TPU v7x, 256 devices: a whole 4x4x8 slice. The times are simulated.
256 devices in a mesh: fsdp: 16 (over x, y), seq: 16 (over z, core).
Axes of the slice: x: 4, y: 4, z: 8, core: 2. Of those that a mesh axis runs over, the one named last changes fastest.
Arguments:
- tokens: bfloat16 [65536, 2048], P(('fsdp', 'seq')), may hold values from -6 to 6
- seq_lengths: int32 [16, 4], P('fsdp'), may hold values from 1 to 2048, 4096 in all within a row
- in_weight: bfloat16 [2048, 6144], P(None, 'fsdp'), may hold values from -0.125 to 0.125
- short_filter: float32 [7, 6144], replicated, may hold values from -2.5 to 2.5
- long_filter: bfloat16 [128, 128], replicated, may hold values from -0.5 to 0.5
- out_weight: bfloat16 [2048, 2048], replicated, may hold values from -0.125 to 0.125
Outputs:
- mixed: bfloat16 [65536, 2048], P(('fsdp', 'seq'))
Inputs may be any that keep to these rules, and one draw needn't show every extreme that they name: `seq_lengths`: in each pack the 4 lengths sum to 4096 and the longest is exactly 2048.
All inputs are finite; a program needn't handle non-finite values.
Results may differ from a plain program's by a relative error of at most 0.0073.
Values may be sent and summed in bfloat16 or wider, within the bound.
No kernel may reach another device: no remote copies, remote signals or barrier semaphores. Data moves between devices by JAX's collectives and lax.ppermute only.
A program may use at most 128 MiB of HBM per device.

v0:
```python
import jax
import jax.numpy as jnp
from jax import lax
from jax.sharding import PartitionSpec as P

LANE = 128
GROUP_DEVS = 4


def positions(row_ids, seq_starts):
    seq_begin = jnp.max(
        jnp.where(seq_starts[None, :] <= row_ids[:, None], seq_starts[None, :], 0), axis=1
    )
    return row_ids - seq_begin


def tap_table(tap_ids, long_filter):
    filter_len = long_filter.shape[0]
    one_hot = (
        tap_ids[:, :, None] == jnp.arange(filter_len, dtype=jnp.int32)[None, None, :]
    ).astype(jnp.bfloat16)
    return jnp.einsum(
        "ijt,tg->gij", one_hot, long_filter, preferred_element_type=jnp.float32
    ).astype(jnp.bfloat16)


def local(tokens, seq_lengths, in_weight, short_filter, long_filter, out_weight):
    rows, channels = tokens.shape
    width = short_filter.shape[0]
    filter_len, group_count = long_filter.shape
    per_group = channels // group_count
    n_seq = lax.axis_size("seq")
    s = lax.axis_index("seq")
    member = s % GROUP_DEVS
    part = LANE // GROUP_DEVS
    n_lblk = channels // LANE
    tail = filter_len + 8
    span = GROUP_DEVS * rows
    ext_rows = tail + span
    swaps = [[(i, i ^ d) for i in range(n_seq)] for d in range(1, GROUP_DEVS)]
    from_member = [tokens, lax.ppermute(tokens, "seq", swaps[0])]
    for d in range(2, GROUP_DEVS, 2):
        fetched = lax.ppermute(tokens, "seq", swaps[d - 1])
        from_member += [fetched, lax.ppermute(fetched, "seq", swaps[0])]
    blocks = []
    for m in range(GROUP_DEVS):
        pick = from_member[0]
        for d in range(1, GROUP_DEVS):
            pick = jnp.where(member ^ d == m, from_member[d], pick)
        blocks.append(pick)
    tail_src = tokens[rows - tail :]
    tail_tok = jnp.zeros_like(tail_src)
    for m in range(GROUP_DEVS):
        dist = m + 1
        perm = [(i - dist, i) for i in range(GROUP_DEVS, n_seq) if i % GROUP_DEVS == m]
        got = lax.ppermute(tail_src, "seq", perm)
        tail_tok = jnp.where(member == m, got, tail_tok)
    ext_tokens = jnp.concatenate([tail_tok] + blocks, axis=0)
    lengths_row = seq_lengths[0]
    seq_starts = jnp.cumsum(lengths_row) - lengths_row
    pair_start = s // GROUP_DEVS * span
    row_ids = pair_start - tail + jnp.arange(ext_rows, dtype=jnp.int32)
    position = positions(row_ids, seq_starts)
    offset = member * part
    w_t = in_weight.T.reshape(in_weight.shape[1] // LANE, LANE, channels)
    w_part = lax.dynamic_slice_in_dim(w_t, offset, part, axis=1)
    w_all = lax.all_gather(w_part, "fsdp", axis=0, tiled=True)
    own = n_lblk * part
    w_all = w_all.reshape(3 * own, channels)
    ow = out_weight.reshape(n_lblk, LANE, channels)
    weights = []
    for d in range(GROUP_DEVS):
        src_offset = (member ^ d) * part
        weights.append(
            lax.dynamic_slice_in_dim(ow, src_offset, part, axis=1).reshape(own, channels)
        )
    ow_cat = jnp.concatenate(weights, axis=0)
    ext_tokens, ow_cat = lax.optimization_barrier((ext_tokens, ow_cat))
    projected = jnp.dot(ext_tokens, w_all.T, preferred_element_type=jnp.float32).astype(
        jnp.bfloat16
    )
    taps = short_filter.reshape(width, 3, n_lblk, LANE)
    taps = lax.dynamic_slice_in_dim(taps, offset, part, axis=3).reshape(width, 3 * own)
    start = 8
    feat_rows = ext_rows - start
    pos_f = position[start:]
    featured = jnp.zeros((feat_rows, 3 * own), jnp.float32)
    for tap_index in range(width):
        shifted = projected[start - tap_index : ext_rows - tap_index].astype(jnp.float32)
        featured = featured + taps[tap_index] * jnp.where(
            (pos_f >= tap_index)[:, None], shifted, 0.0
        )
    queries = featured[feat_rows - span :, :own]
    mixed_in = (featured[:, own : 2 * own] * featured[:, 2 * own :]).astype(jnp.bfloat16)
    sub = LANE // per_group
    lf = long_filter.reshape(filter_len, n_lblk, sub)
    lf = lax.dynamic_slice_in_dim(lf, offset // per_group, part // per_group, axis=2)
    lf = lf.reshape(filter_len, own // per_group)
    n_groups = own // per_group
    out_rows = jnp.arange(filter_len, dtype=jnp.int32)[:, None]
    src_rows = jnp.arange(filter_len, dtype=jnp.int32)[None, :]
    cur_tap = out_rows - src_rows
    prev_tap = out_rows + filter_len - src_rows
    cur_table = tap_table(cur_tap, lf)
    prev_table = tap_table(prev_tap, lf)
    n_blocks = span // filter_len
    pos_out = position[tail:].reshape(n_blocks, filter_len)
    cur_kernel = jnp.where(
        (cur_tap[None] <= pos_out[:, :, None])[:, None], cur_table[None], 0.0
    ).astype(jnp.bfloat16)
    prev_kernel = jnp.where(
        (prev_tap[None] <= pos_out[:, :, None])[:, None], prev_table[None], 0.0
    ).astype(jnp.bfloat16)
    mi_t = mixed_in.T.reshape(n_groups, per_group, n_blocks + 1, filter_len)
    filtered = jnp.einsum(
        "gcbj,bgij->gcbi", mi_t[:, :, 1:], cur_kernel, preferred_element_type=jnp.float32
    )
    filtered = filtered + jnp.einsum(
        "gcbj,bgij->gcbi", mi_t[:, :, :-1], prev_kernel, preferred_element_type=jnp.float32
    )
    filtered = filtered.reshape(own, span)
    gated = (queries.T * filtered).astype(jnp.bfloat16)
    gated = gated.T.reshape(GROUP_DEVS, rows, own)
    pieces = []
    for d in range(GROUP_DEVS):
        send = lax.dynamic_index_in_dim(gated, member ^ d, axis=0, keepdims=False)
        got = send if d == 0 else lax.ppermute(send, "seq", swaps[d - 1])
        pieces.append(got)
    result = tokens.astype(jnp.float32) + jnp.dot(
        jnp.concatenate(pieces, axis=1), ow_cat, preferred_element_type=jnp.float32
    )
    return result.astype(jnp.bfloat16)


def solution(mesh):
    in_specs = (P(("fsdp", "seq"), None), P("fsdp", None), P(None, "fsdp"), P(), P(), P())
    out_specs = P(("fsdp", "seq"), None)
    return jax.shard_map(local, mesh=mesh, in_specs=in_specs, out_specs=out_specs, check_vma=False)
```

profile of v0, /device:TPU:1, one launch (start us, length us, event | category | flops | bytes accessed | tf_op | source)
XLA Modules:
  0.0 154.7 jit_solution(10799367417863991124)
XLA Ops:
  6.5 1.8 %copy.26 = bf16[2048,384]{0,1:T(8,128)(2,1)S(1)} copy(bf16[2048,384]{1,0:T(8,128)(2,1)} %param.8) | data formatting | bytes 3145728 | tf_op args[2]
  15.4 8.6 %collective-permute-start.4 = (bf16[256,2048]{1,0:T(8,128)(2,1)S(1)}, bf16[256,2048]{1,0:T(8,128)(2,1)S(1)}, u32[]{:S(2)}, u32[]{:S(2)}) collective-permute-start(bf16[256,2048]{1,0:T(8,128)(2,1)S(1)} %copy-done.1), channel_id=1, source_target_pairs={{0,2},{1,3},{2,0},{3,1},{4,6},{5,7},{6,4},{7,5},{8,10},{9,11},{10,... | collective-permute-start | bytes 3145736 | tf_op jit(solution)/shard_map/ppermute | solution.py:43
  27.4 4.0 %fusion.20 = bf16[32,128,128]{2,0,1:T(8,128)(2,1)S(1)} fusion(bf16[128,32,1]{0,1,2:T(8,128)(2,1)S(1)} %bitcast.77, s32[128,128]{1,0:T(8,128)S(1)} %get-tuple-element.35), kind=kOutput, calls=%fused_computation.28 | convolution fusion | flops 136839168 | bytes 1122304 | tf_op jit(solution)/shard_map/ijt,tg->gij/dot_general | solution.py:22
  32.8 3.9 %fusion.21 = bf16[32,128,128]{2,0,1:T(8,128)(2,1)S(1)} fusion(bf16[128,32,1]{0,1,2:T(8,128)(2,1)S(1)} %bitcast.78, s32[128,128]{1,0:T(8,128)S(1)} %get-tuple-element.36), kind=kOutput, calls=%fused_computation.29 | convolution fusion | flops 136839168 | bytes 1122304 | tf_op jit(solution)/shard_map/ijt,tg->gij/dot_general | solution.py:22
  39.2 4.3 %constant_dynamic-slice_fusion.11 = (bf16[16,32,2048]{2,1,0:T(8,128)(2,1)S(1)}, bf16[16,32,2048]{2,1,0:T(8,128)(2,1)S(1)}, bf16[16,32,2048]{2,1,0:T(8,128)(2,1)S(1)}, bf16[16,32,2048]{2,1,0:T(8,128)(2,1)S(1)}) fusion(bf16[16,128,2048]{2,1,0:T(8,128)(2,1)} %bitcast.65, s32[]{:T(128)S(6)} %select_n.178, s32[]{:T(128)S(6)} %select_n.215, s32[]{:T(128)S(6)} %select_n.214, ...), kind=kLoop, calls=%fused_computation.73 | loop fusion | bytes 16777232 | tf_op jit(solution)/shard_map/dynamic_slice | solution.py:75
  44.2 4.1 %pad_maximum_fusion = bf16[2048,2048]{1,0:T(8,128)(2,1)} fusion(bf16[512,2048]{1,0:T(8,128)(2,1)S(1)} %bitcast.69, bf16[512,2048]{1,0:T(8,128)(2,1)S(1)} %bitcast.70, bf16[512,2048]{1,0:T(8,128)(2,1)S(1)} %bitcast.71, bf16[512,2048]{1,0:T(8,128)(2,1)S(1)} %bitcast.68), kind=kLoop, calls=%fused_computation | loop fusion | flops 33554432 | bytes 16777216 | tf_op jit(solution)/shard_map/concatenate | solution.py:77
  48.3 2.3 %select_dynamic-update-slice_fusion.4 = bf16[1160,2048]{1,0:T(8,128)(2,1)} fusion(bf16[136,2048]{1,0:T(8,128)(2,1)S(1)} %collective-permute-done, bf16[136,2048]{1,0:T(8,128)(2,1)} %collective-permute-done.1, bf16[136,2048]{1,0:T(8,128)(2,1)} %collective-permute-done.2, bf16[136,2048]{1,0:T(8,128)(2,1)} %collective-permute-done.3, pred[]{:T(512)S(6)} %eq.79, ...), kind=kLoop, calls=%fused_computation.44 | loop fusion | flops 1114111 | bytes 2785284
  50.6 1.7 %select_dynamic-update-slice_fusion.3 = bf16[1160,2048]{1,0:T(8,128)(2,1)} fusion(bf16[1160,2048]{1,0:T(8,128)(2,1)} %select_dynamic-update-slice_fusion.4, bf16[256,2048]{1,0:T(8,128)(2,1)S(1)} %collective-permute-done.5, bf16[256,2048]{1,0:T(8,128)(2,1)S(1)} %collective-permute-done.4, bf16[256,2048]{1,0:T(8,128)(2,1)S(1)} %collective-permute-done.6, ...), kind=kLoop, calls=%fused_computation.43 | loop fusion | flops 1572864 | bytes 5242883
  52.3 1.7 %select_dynamic-update-slice_fusion.2 = bf16[1160,2048]{1,0:T(8,128)(2,1)} fusion(bf16[1160,2048]{1,0:T(8,128)(2,1)} %select_dynamic-update-slice_fusion.3, bf16[256,2048]{1,0:T(8,128)(2,1)S(1)} %collective-permute-done.5, bf16[256,2048]{1,0:T(8,128)(2,1)S(1)} %collective-permute-done.4, bf16[256,2048]{1,0:T(8,128)(2,1)S(1)} %collective-permute-done.6, ...), kind=kLoop, calls=%fused_computation.42 | loop fusion | flops 1572864 | bytes 5242883
  54.0 1.7 %select_dynamic-update-slice_fusion.1 = bf16[1160,2048]{1,0:T(8,128)(2,1)} fusion(bf16[1160,2048]{1,0:T(8,128)(2,1)} %select_dynamic-update-slice_fusion.2, bf16[256,2048]{1,0:T(8,128)(2,1)S(1)} %collective-permute-done.5, bf16[256,2048]{1,0:T(8,128)(2,1)S(1)} %collective-permute-done.4, bf16[256,2048]{1,0:T(8,128)(2,1)S(1)} %collective-permute-done.6, ...), kind=kLoop, calls=%fused_computation.41 | loop fusion | flops 1572864 | bytes 5242883
  55.7 1.7 %select_dynamic-update-slice_fusion = bf16[1160,2048]{1,0:T(8,128)(2,1)} fusion(bf16[1160,2048]{1,0:T(8,128)(2,1)} %select_dynamic-update-slice_fusion.1, bf16[256,2048]{1,0:T(8,128)(2,1)S(1)} %collective-permute-done.5, bf16[256,2048]{1,0:T(8,128)(2,1)S(1)} %collective-permute-done.4, bf16[256,2048]{1,0:T(8,128)(2,1)S(1)} %collective-permute-done.6, ...), kind=kLoop, calls=%fused_computation.40 | loop fusion | flops 1572864 | bytes 5242883 | tf_op jit(solution)/shard_map/concatenate | solution.py:58
  57.4 22.7 %all-gather.2.cloned.1.call-done = bf16[48,32,2048]{2,1,0:T(8,128)(2,1)} async-done(((bf16[3,32,2048]{2,1,0:T(8,128)(2,1)}), bf16[48,32,2048]{2,1,0:T(8,128)(2,1)}) %all-gather.2.cloned.1.call-update) | async-done | bytes 6291472 | tf_op jit(solution)/shard_map/all_gather | solution.py:67
  80.1 11.2 %convolution_convert_fusion = bf16[1160,1536]{1,0:T(8,128)(2,1)S(1)} fusion(bf16[1160,2048]{1,0:T(8,128)(2,1)} %select_dynamic-update-slice_fusion, bf16[1536,2048]{1,0:T(8,128)(2,1)} %bitcast.79), kind=kOutput, calls=%fused_computation.11 | convolution fusion | flops 7299870720 | bytes 14606336 | tf_op jit(solution)/shard_map/dot_general | solution.py:79
  91.2 10.7 %multiply_add_fusion = f32[1152,1536]{1,0:T(8,128)S(1)} fusion(bf16[1160,1536]{1,0:T(8,128)(2,1)S(1)} %convolution_convert_fusion, f32[1536]{0:T(1024)S(1)} %mul.115, f32[1536]{0:T(1024)S(1)} %mul.112, f32[1536]{0:T(1024)S(1)} %mul.109, f32[1536]{0:T(1024)S(1)} %mul.106, f32[1536]{0:T(1024)S(1)} %mul.103, f32[1536]{0:T(1024)S(1)} %mul.100, ...), kind=kLoop, calls=%fused_computation.12 | loop fusion | flops 47775744 | bytes 31901568 | tf_op jit(solution)/shard_map/add | solution.py:90
  101.9 2.9 %copy-done = f32[1152,1536]{1,0:T(8,128)} copy-done((f32[1152,1536]{1,0:T(8,128)}, f32[1152,1536]{1,0:T(8,128)S(1)}, u32[]{:S(2)}) %copy-start) | copy-done | bytes 7077912
  106.7 2.7 %reshape.154 = bf16[32,16,9,128]{3,2,1,0:T(8,128)(2,1)S(1)} reshape(bf16[512,1152]{1,0:T(8,128)(2,1)} %copy.29) | data formatting | bytes 2359296 | tf_op jit(solution)/shard_map/reshape | solution.py:114
  109.9 5.8 %fusion = f32[32,8,128,16]{2,3,1,0:T(8,128)S(1)} fusion(pred[8,128,128]{2,1,0:T(8,128)(4,1)S(1)} %copy-done.3, bf16[32,128,128]{2,1,0:T(8,128)(2,1)} %copy.31, bf16[32,16,8,128]{3,2,1,0:T(8,128)(2,1)S(1)} %get-tuple-element.14), kind=kOutput, calls=%fused_computation.1 | convolution fusion | flops 138412032 | bytes 4325376 | tf_op jit(solution)/shard_map/gcbj,bgij->gcbi/dot_general | solution.py:118
  115.6 4.5 %add_bitcast_fusion = f32[32,16,8,128]{3,1,2,0:T(8,128)S(1)} fusion(f32[32,8,128,16]{2,3,1,0:T(8,128)S(1)} %fusion, pred[8,128,128]{2,1,0:T(8,128)(4,1)S(1)} %get-tuple-element.33, bf16[32,128,128]{2,1,0:T(8,128)(2,1)S(1)} %copy-done.2, bf16[32,16,8,128]{3,2,1,0:T(8,128)(2,1)S(1)} %get-tuple-element.13), kind=kOutput, calls=%fused_computation.27 | convolution fusion | flops 138936320 | bytes 6422528 | tf_op jit(solution)/shard_map/gcbj,bgij->gcbi/dot_general | solution.py:115
  121.0 1.8 %copy.44 = f32[64,8,8,128]{3,1,2,0:T(8,128)} copy(f32[64,8,8,128]{3,2,1,0:T(8,128)S(1)} %bitcast.66) | data formatting | bytes 4194304
  122.8 1.9 %copy.34 = f32[512,1024]{0,1:T(8,128)S(1)} copy(f32[512,1024]{1,0:T(8,128)} %bitcast.67) | data formatting | bytes 4194304 | tf_op jit(solution)/shard_map/reshape | solution.py:121
  124.7 1.9 %fusion.17 = bf16[512,1024]{0,1:T(8,128)(2,1)S(1)} fusion(f32[512,1024]{0,1:T(8,128)S(1)} %copy.34, f32[1152,1536]{1,0:T(8,128)} %copy-done), kind=kLoop, calls=%fused_computation.26 | loop fusion | flops 1048576 | bytes 5242880 | tf_op jit(solution)/shard_map/convert_element_type | solution.py:122
  129.2 6.1 %collective-permute-done.8 = bf16[256,512]{1,0:T(8,128)(2,1)S(1)} collective-permute-done((bf16[256,512]{1,0:T(8,128)(2,1)S(1)}, bf16[256,512]{1,0:T(8,128)(2,1)S(1)}, u32[]{:S(2)}, u32[]{:S(2)}) %collective-permute-start.8) | collective-permute-done | bytes 262176 | tf_op jit(solution)/shard_map/ppermute | solution.py:127
  135.4 5.8 %collective-permute-done.9 = bf16[256,512]{1,0:T(8,128)(2,1)S(1)} collective-permute-done((bf16[256,512]{1,0:T(8,128)(2,1)S(1)}, bf16[256,512]{1,0:T(8,128)(2,1)S(1)}, u32[]{:S(2)}, u32[]{:S(2)}) %collective-permute-start.9) | collective-permute-done | bytes 262176 | tf_op jit(solution)/shard_map/ppermute | solution.py:127
  141.2 6.7 %fusion.14 = bf16[256,2048]{1,0:T(8,128)(2,1)} fusion(bf16[2048,2048]{1,0:T(8,128)(2,1)} %pad_maximum_fusion, bf16[256,2048]{1,0:T(8,128)(2,1)S(1)} %copy-done.1, bf16[256,512]{1,0:T(8,128)(2,1)S(1)} %collective-permute-done.9, bf16[256,512]{1,0:T(8,128)(2,1)S(1)} %collective-permute-done.8, bf16[256,512]{1,0:T(8,128)(2,1)S(1)} %collective-permute-done.7, ...), kind=kOutput, calls=%fused_computation.20 | convolution fusion | flops 2153250816 | bytes 11534336 | tf_op jit(solution)/shard_map/dot_general | solution.py:129
  (58 shorter events, 20.6 us)
Async XLA Ops:
  6.5 8.8 %copy-start.1 = (bf16[256,2048]{1,0:T(8,128)(2,1)S(1)}, bf16[256,2048]{1,0:T(8,128)(2,1)}, u32[]{:S(2)}) copy-start(bf16[256,2048]{1,0:T(8,128)(2,1)} %param.6) | copy-start | bytes 3145732
  6.5 73.5 %all-gather.2.cloned.1.call-start = ((), (), s32[]{:S(2)}) async-start(), calls=%async_computation | async-start | bytes 6684672 | tf_op jit(solution)/shard_map/all_gather | solution.py:67
  10.3 33.3 %collective-permute-start = (bf16[136,2048]{1,0:T(8,128)(2,1)S(1)}, bf16[136,2048]{1,0:T(8,128)(2,1)S(1)}, u32[]{:S(2)}, u32[]{:S(2)}) collective-permute-start(bf16[136,2048]{1,0:T(8,128)(2,1)S(1)} %slice.75), channel_id=1, source_target_pairs={{3,7},{7,11},{11,15},{19,23},{23,27},{27,31},{35,39},{39,43},{43,4... | collective-permute-start | bytes 1671176 | tf_op jit(solution)/shard_map/ppermute | solution.py:56
  11.0 37.3 %collective-permute-start.1 = (bf16[136,2048]{1,0:T(8,128)(2,1)S(1)}, bf16[136,2048]{1,0:T(8,128)(2,1)}, u32[]{:S(2)}, u32[]{:S(2)}) collective-permute-start(bf16[136,2048]{1,0:T(8,128)(2,1)S(1)} %slice.75), channel_id=1, source_target_pairs={{3,6},{7,10},{11,14},{19,22},{23,26},{27,30},{35,38},{39,42},{43,4... | collective-permute-start | bytes 1671176 | tf_op jit(solution)/shard_map/ppermute | solution.py:56
  12.4 35.8 %collective-permute-start.2 = (bf16[136,2048]{1,0:T(8,128)(2,1)S(1)}, bf16[136,2048]{1,0:T(8,128)(2,1)}, u32[]{:S(2)}, u32[]{:S(2)}) collective-permute-start(bf16[136,2048]{1,0:T(8,128)(2,1)S(1)} %slice.75), channel_id=1, source_target_pairs={{3,5},{7,9},{11,13},{19,21},{23,25},{27,29},{35,37},{39,41},{43,45... | collective-permute-start | bytes 1671176 | tf_op jit(solution)/shard_map/ppermute | solution.py:56
  13.9 34.4 %collective-permute-start.3 = (bf16[136,2048]{1,0:T(8,128)(2,1)S(1)}, bf16[136,2048]{1,0:T(8,128)(2,1)}, u32[]{:S(2)}, u32[]{:S(2)}) collective-permute-start(bf16[136,2048]{1,0:T(8,128)(2,1)S(1)} %slice.75), channel_id=1, source_target_pairs={{3,4},{7,8},{11,12},{19,20},{23,24},{27,28},{35,36},{39,40},{43,44... | collective-permute-start | bytes 1671176 | tf_op jit(solution)/shard_map/ppermute | solution.py:56
  15.4 28.6 %collective-permute-start.4 = (bf16[256,2048]{1,0:T(8,128)(2,1)S(1)}, bf16[256,2048]{1,0:T(8,128)(2,1)S(1)}, u32[]{:S(2)}, u32[]{:S(2)}) collective-permute-start(bf16[256,2048]{1,0:T(8,128)(2,1)S(1)} %copy-done.1), channel_id=1, source_target_pairs={{0,2},{1,3},{2,0},{3,1},{4,6},{5,7},{6,4},{7,5},{8,10},{9,11},{10,... | collective-permute-start | bytes 3145736 | tf_op jit(solution)/shard_map/ppermute | solution.py:43
  25.5 12.6 %copy-start.4 = (s32[1,4]{1,0:T(1,128)S(1)}, s32[1,4]{1,0:T(1,128)}, u32[]{:S(2)}) copy-start(s32[1,4]{1,0:T(1,128)} %param.7) | copy-start | bytes 52
  43.6 7.0 %collective-permute-start.6 = (bf16[256,2048]{1,0:T(8,128)(2,1)S(1)}, bf16[256,2048]{1,0:T(8,128)(2,1)S(1)}, u32[]{:S(2)}, u32[]{:S(2)}) collective-permute-start(bf16[256,2048]{1,0:T(8,128)(2,1)S(1)} %copy-done.1), channel_id=1, source_target_pairs={{0,1},{1,0},{2,3},{3,2},{4,5},{5,4},{6,7},{7,6},{8,9},{9,8},{10,11... | collective-permute-start | bytes 3145736 | tf_op jit(solution)/shard_map/ppermute | solution.py:41
  44.0 6.6 %collective-permute-start.5 = (bf16[256,2048]{1,0:T(8,128)(2,1)S(1)}, bf16[256,2048]{1,0:T(8,128)(2,1)S(1)}, u32[]{:S(2)}, u32[]{:S(2)}) collective-permute-start(bf16[256,2048]{1,0:T(8,128)(2,1)S(1)} %collective-permute-done.4), channel_id=1, source_target_pairs={{0,1},{1,0},{2,3},{3,2},{4,5},{5,4},{6,7},{7,6},{8,9},{9,8},{10,11... | collective-permute-start | bytes 3145736 | tf_op jit(solution)/shard_map/ppermute | solution.py:44
  101.9 2.9 %copy-start = (f32[1152,1536]{1,0:T(8,128)}, f32[1152,1536]{1,0:T(8,128)S(1)}, u32[]{:S(2)}) copy-start(f32[1152,1536]{1,0:T(8,128)S(1)} %multiply_add_fusion) | copy-start | bytes 21233668
  105.3 4.6 %copy-start.3 = (pred[8,128,128]{2,1,0:T(8,128)(4,1)S(1)}, pred[8,128,128]{2,1,0:T(8,128)(4,1)}, u32[]{:S(2)}) copy-start(pred[8,128,128]{2,1,0:T(8,128)(4,1)} %get-tuple-element.34) | copy-start | bytes 393220
  109.9 5.8 %copy-start.2 = (bf16[32,128,128]{2,1,0:T(8,128)(2,1)S(1)}, bf16[32,128,128]{2,1,0:T(8,128)(2,1)}, u32[]{:S(2)}) copy-start(bf16[32,128,128]{2,1,0:T(8,128)(2,1)} %copy.28) | copy-start | bytes 3145732
  126.7 2.5 %collective-permute-start.7 = (bf16[256,512]{1,0:T(8,128)(2,1)S(1)}, bf16[256,512]{1,0:T(8,128)(2,1)S(1)}, u32[]{:S(2)}, u32[]{:S(2)}) collective-permute-start(bf16[256,512]{1,0:T(8,128)(2,1)S(1)} %get-tuple-element.18), channel_id=1, source_target_pairs={{0,1},{1,0},{2,3},{3,2},{4,5},{5,4},{6,7},{7,6},{8,9},{9,8},{10,11... | collective-permute-start | bytes 786440 | tf_op jit(solution)/shard_map/ppermute | solution.py:127
  127.5 7.9 %collective-permute-start.8 = (bf16[256,512]{1,0:T(8,128)(2,1)S(1)}, bf16[256,512]{1,0:T(8,128)(2,1)S(1)}, u32[]{:S(2)}, u32[]{:S(2)}) collective-permute-start(bf16[256,512]{1,0:T(8,128)(2,1)S(1)} %get-tuple-element.17), channel_id=1, source_target_pairs={{0,2},{1,3},{2,0},{3,1},{4,6},{5,7},{6,4},{7,5},{8,10},{9,11},{10,... | collective-permute-start | bytes 786440 | tf_op jit(solution)/shard_map/ppermute | solution.py:127
  128.8 12.4 %collective-permute-start.9 = (bf16[256,512]{1,0:T(8,128)(2,1)S(1)}, bf16[256,512]{1,0:T(8,128)(2,1)S(1)}, u32[]{:S(2)}, u32[]{:S(2)}) collective-permute-start(bf16[256,512]{1,0:T(8,128)(2,1)S(1)} %get-tuple-element.16), channel_id=1, source_target_pairs={{0,3},{1,2},{2,1},{3,0},{4,7},{5,6},{6,5},{7,4},{8,11},{9,10},{10,... | collective-permute-start | bytes 786440 | tf_op jit(solution)/shard_map/ppermute | solution.py:127
Sparse Core Ops, SparseCore 0:
  9.8 70.1 all-gather.1
where the time goes:
time: 155 us
  matrix products  36 us (23%)
  waiting for transfers between devices  34.9 us (23%)
  other arithmetic  28.2 us (18%)
  local copies, waits for them, and re-layouts  25.5 us (16%)
  starting transfers between devices  16.5 us (11%)
  between operations  13.6 us (9%)
    all_gather x1, waiting for transfers between devices, local(): w_all = lax.all_gather(w_part, 'fsdp', axis=0, tiled=True)  22.7 us
    ppermute x3, waiting for transfers between devices, local(): got = send if d == 0 else lax.ppermute(send, 'seq', swaps[d - 1])  11.9 us
    dot_general x1, matrix products, local(): jnp.dot(ext_tokens, w_all.T, preferred_element_type=jnp.float32)  11.2 us
    add x1, other arithmetic, local(): featured + taps[tap_index] * jnp.where((pos_f >= tap_index)[:, None], shi...  10.7 us
    ppermute x1, starting transfers between devices, local(): fetched = lax.ppermute(tokens, 'seq', swaps[d - 1])  8.59 us
    unnamed x14, local copies, waits for them, and re-layouts  8.3 us
    dot_general x2, matrix products, tap_table(): jnp.einsum('ijt,tg->gij', one_hot, long_filter, preferred_element_type=jn...  7.92 us
    unnamed x4, other arithmetic  7.39 us
  transfers between devices with their start and end apart: 11, of which 4 were waited for; matrix products, arithmetic and copies ran while one was open for 22% of the time, Pallas kernels for 0%

commit v1 on v0

--- a/solution.py
+++ b/solution.py
@@ -64,7 +64,8 @@
     offset = member * part
     w_t = in_weight.T.reshape(in_weight.shape[1] // LANE, LANE, channels)
     w_part = lax.dynamic_slice_in_dim(w_t, offset, part, axis=1)
-    w_all = lax.all_gather(w_part, "fsdp", axis=0, tiled=True)
+    sent = jnp.stack([w_part] * lax.axis_size("fsdp"))
+    w_all = jnp.concatenate(lax.all_to_all(sent, "fsdp", 0, 0), axis=0)
     own = n_lblk * part
     w_all = w_all.reshape(3 * own, channels)
     ow = out_weight.reshape(n_lblk, LANE, channels)

time: 155 us -> 204 us (1.32)
  the two profiles are of different devices: /device:TPU:1 before, /device:TPU:221 now
where the time goes in v1:
time: 204 us; the launch traced here: 203 us
  waiting for transfers between devices  91.9 us (45%)
  matrix products  36 us (18%)
  local copies, waits for them, and re-layouts  29.2 us (14%)
  other arithmetic  28.5 us (14%)
  starting transfers between devices  17.5 us (9%)
    all_to_all x1, waiting for transfers between devices, local(): w_all = jnp.concatenate(lax.all_to_all(sent, 'fsdp', 0, 0), axis=0)  77.1 us
    ppermute x3, waiting for transfers between devices, local(): got = send if d == 0 else lax.ppermute(send, 'seq', swaps[d - 1])  11.9 us
    dot_general x1, matrix products, local(): jnp.dot(ext_tokens, w_all.T, preferred_element_type=jnp.float32)  11.2 us
    add x1, other arithmetic, local(): featured + taps[tap_index] * jnp.where((pos_f >= tap_index)[:, None], shi...  10.7 us
    dot_general x2, matrix products, tap_table(): jnp.einsum('ijt,tg->gij', one_hot, long_filter, preferred_element_type=jn...  7.91 us
    unnamed x4, other arithmetic  7.36 us
    all_to_all x1, starting transfers between devices, local(): w_all = jnp.concatenate(lax.all_to_all(sent, 'fsdp', 0, 0), axis=0)  6.68 us
    dot_general x1, matrix products, local(): jnp.dot(jnp.concatenate(pieces, axis=1), ow_cat, preferred_element_type=j...  6.68 us
  transfers between devices with their start and end apart: 11, of which 4 were waited for; matrix products, arithmetic and copies ran while one was open for 17% of the time, Pallas kernels for 0%

profile of v1, /device:TPU:221, one launch (start us, length us, event | category | flops | bytes accessed | tf_op | source)
XLA Modules:
  0.0 203.5 jit_solution(12377657766877101748)
XLA Ops:
  0.0 1.9 slice.75
  10.1 3.4 %stack.2 = bf16[16,3,32,2048]{3,2,1,0:T(8,128)(2,1)} broadcast(bf16[3,32,2048]{2,1,0:T(8,128)(2,1)S(1)} %constant_dynamic-slice_fusion.7), dimensions={1,2,3} | broadcast | bytes 6684672 | tf_op jit(solution)/shard_map/stack | solution.py:67
  13.5 6.7 %all-to-all-start = ((bf16[16,3,32,2048]{3,2,1,0:T(8,128)(2,1)}), bf16[16,3,32,2048]{3,2,1,0:T(8,128)(2,1)}, u32[]{:S(2)}, u32[]{:S(2)}) async-start(bf16[16,3,32,2048]{3,2,1,0:T(8,128)(2,1)} %stack.2), calls=%async_computation | async-start | bytes 12582912 | tf_op jit(solution)/shard_map/all_to_all | solution.py:68
  21.3 4.0 %fusion.20 = bf16[32,128,128]{2,0,1:T(8,128)(2,1)S(1)} fusion(bf16[128,32,1]{0,1,2:T(8,128)(2,1)S(1)} %bitcast.77, s32[128,128]{1,0:T(8,128)S(1)} %get-tuple-element.35), kind=kOutput, calls=%fused_computation.28 | convolution fusion | flops 136839168 | bytes 1122304 | tf_op jit(solution)/shard_map/ijt,tg->gij/dot_general | solution.py:22
  26.7 3.9 %fusion.21 = bf16[32,128,128]{2,0,1:T(8,128)(2,1)S(1)} fusion(bf16[128,32,1]{0,1,2:T(8,128)(2,1)S(1)} %bitcast.78, s32[128,128]{1,0:T(8,128)S(1)} %get-tuple-element.36), kind=kOutput, calls=%fused_computation.29 | convolution fusion | flops 136839168 | bytes 1122304 | tf_op jit(solution)/shard_map/ijt,tg->gij/dot_general | solution.py:22
  32.5 4.4 %constant_dynamic-slice_fusion.11 = (bf16[16,32,2048]{2,1,0:T(8,128)(2,1)S(1)}, bf16[16,32,2048]{2,1,0:T(8,128)(2,1)S(1)}, bf16[16,32,2048]{2,1,0:T(8,128)(2,1)S(1)}, bf16[16,32,2048]{2,1,0:T(8,128)(2,1)S(1)}) fusion(bf16[16,128,2048]{2,1,0:T(8,128)(2,1)} %bitcast.65, s32[]{:T(128)S(6)} %select_n.178, s32[]{:T(128)S(6)} %select_n.215, s32[]{:T(128)S(6)} %select_n.214, ...), kind=kLoop, calls=%fused_computation.73 | loop fusion | bytes 16777232 | tf_op jit(solution)/shard_map/dynamic_slice | solution.py:76
  37.8 2.8 %collective-permute-done.4 = bf16[256,2048]{1,0:T(8,128)(2,1)S(1)} collective-permute-done((bf16[256,2048]{1,0:T(8,128)(2,1)}, bf16[256,2048]{1,0:T(8,128)(2,1)S(1)}, u32[]{:S(2)}, u32[]{:S(2)}) %collective-permute-start.4) | collective-permute-done | bytes 1048608 | tf_op jit(solution)/shard_map/ppermute | solution.py:43
  41.1 4.1 %pad_maximum_fusion = bf16[2048,2048]{1,0:T(8,128)(2,1)} fusion(bf16[512,2048]{1,0:T(8,128)(2,1)S(1)} %bitcast.69, bf16[512,2048]{1,0:T(8,128)(2,1)S(1)} %bitcast.70, bf16[512,2048]{1,0:T(8,128)(2,1)S(1)} %bitcast.71, bf16[512,2048]{1,0:T(8,128)(2,1)S(1)} %bitcast.68), kind=kLoop, calls=%fused_computation | loop fusion | flops 33554432 | bytes 16777216 | tf_op jit(solution)/shard_map/concatenate | solution.py:78
  45.2 2.3 %select_dynamic-update-slice_fusion.4 = bf16[1160,2048]{1,0:T(8,128)(2,1)} fusion(bf16[136,2048]{1,0:T(8,128)(2,1)S(1)} %collective-permute-done, bf16[136,2048]{1,0:T(8,128)(2,1)} %collective-permute-done.1, bf16[136,2048]{1,0:T(8,128)(2,1)} %collective-permute-done.2, bf16[136,2048]{1,0:T(8,128)(2,1)} %collective-permute-done.3, pred[]{:T(512)S(6)} %eq.79, ...), kind=kLoop, calls=%fused_computation.44 | loop fusion | flops 1114111 | bytes 2785284
  52.5 1.7 select_dynamic-update-slice_fusion
  54.3 77.1 %all-to-all-done = bf16[16,3,32,2048]{3,2,1,0:T(8,128)(2,1)} async-done(((bf16[16,3,32,2048]{3,2,1,0:T(8,128)(2,1)}), bf16[16,3,32,2048]{3,2,1,0:T(8,128)(2,1)}, u32[]{:S(2)}, u32[]{:S(2)}) %all-to-all-start) | async-done | bytes 6291488 | tf_op jit(solution)/shard_map/all_to_all | solution.py:68
  131.4 11.2 %convolution_convert_fusion = bf16[1160,1536]{1,0:T(8,128)(2,1)S(1)} fusion(bf16[1160,2048]{1,0:T(8,128)(2,1)} %select_dynamic-update-slice_fusion, bf16[1536,2048]{1,0:T(8,128)(2,1)} %bitcast.8), kind=kOutput, calls=%fused_computation.11 | convolution fusion | flops 7299870720 | bytes 14606336 | tf_op jit(solution)/shard_map/dot_general | solution.py:80
  142.5 10.7 %multiply_add_fusion = f32[1152,1536]{1,0:T(8,128)S(1)} fusion(bf16[1160,1536]{1,0:T(8,128)(2,1)S(1)} %convolution_convert_fusion, f32[1536]{0:T(1024)S(1)} %mul.115, f32[1536]{0:T(1024)S(1)} %mul.112, f32[1536]{0:T(1024)S(1)} %mul.109, f32[1536]{0:T(1024)S(1)} %mul.106, f32[1536]{0:T(1024)S(1)} %mul.103, f32[1536]{0:T(1024)S(1)} %mul.100, ...), kind=kLoop, calls=%fused_computation.12 | loop fusion | flops 47775744 | bytes 31901568 | tf_op jit(solution)/shard_map/add | solution.py:91
  153.2 2.9 %copy-done = f32[1152,1536]{1,0:T(8,128)} copy-done((f32[1152,1536]{1,0:T(8,128)}, f32[1152,1536]{1,0:T(8,128)S(1)}, u32[]{:S(2)}) %copy-start) | copy-done | bytes 7077912
  160.9 2.3 %fusion.36 = (bf16[32,16,8,128]{3,2,1,0:T(8,128)(2,1)S(1)}, bf16[32,16,8,128]{3,2,1,0:T(8,128)(2,1)S(1)}) fusion(bf16[32,16,9,128]{3,2,1,0:T(8,128)(2,1)} %reshape.152), kind=kLoop, calls=%fused_computation.82 | loop fusion | bytes 4194304 | tf_op jit(solution)/shard_map/slice | solution.py:117
  163.2 5.8 %fusion = f32[32,8,128,16]{2,3,1,0:T(8,128)S(1)} fusion(pred[8,128,128]{2,1,0:T(8,128)(4,1)S(1)} %get-tuple-element.34, bf16[32,128,128]{2,1,0:T(8,128)(2,1)} %copy.23, bf16[32,16,8,128]{3,2,1,0:T(8,128)(2,1)S(1)} %get-tuple-element.14), kind=kOutput, calls=%fused_computation.1 | convolution fusion | flops 138412032 | bytes 4325376 | tf_op jit(solution)/shard_map/gcbj,bgij->gcbi/dot_general | solution.py:119
  169.0 4.5 %add_bitcast_fusion = f32[32,16,8,128]{3,1,2,0:T(8,128)S(1)} fusion(f32[32,8,128,16]{2,3,1,0:T(8,128)S(1)} %fusion, pred[8,128,128]{2,1,0:T(8,128)(4,1)S(1)} %get-tuple-element.33, bf16[32,128,128]{2,1,0:T(8,128)(2,1)S(1)} %copy-done.2, bf16[32,16,8,128]{3,2,1,0:T(8,128)(2,1)S(1)} %get-tuple-element.13), kind=kOutput, calls=%fused_computation.27 | convolution fusion | flops 138936320 | bytes 6422528 | tf_op jit(solution)/shard_map/gcbj,bgij->gcbi/dot_general | solution.py:116
  174.4 1.8 copy.36
  176.2 2.9 %copy.26 = f32[512,1024]{0,1:T(8,128)} copy(f32[512,1024]{1,0:T(8,128)} %bitcast.67) | data formatting | bytes 4194304 | tf_op jit(solution)/shard_map/reshape | solution.py:122
  179.0 2.6 %fusion.17 = bf16[512,1024]{0,1:T(8,128)(2,1)S(1)} fusion(f32[512,1024]{0,1:T(8,128)} %copy.26, f32[1152,1536]{1,0:T(8,128)} %copy-done), kind=kLoop, calls=%fused_computation.26 | loop fusion | flops 1048576 | bytes 5242880 | tf_op jit(solution)/shard_map/convert_element_type | solution.py:123
  183.1 1.7 collective-permute-start.9
  184.9 6.1 %collective-permute-done.8 = bf16[256,512]{1,0:T(8,128)(2,1)S(1)} collective-permute-done((bf16[256,512]{1,0:T(8,128)(2,1)S(1)}, bf16[256,512]{1,0:T(8,128)(2,1)S(1)}, u32[]{:S(2)}, u32[]{:S(2)}) %collective-permute-start.8) | collective-permute-done | bytes 262176 | tf_op jit(solution)/shard_map/ppermute | solution.py:128
  191.0 5.8 %collective-permute-done.9 = bf16[256,512]{1,0:T(8,128)(2,1)S(1)} collective-permute-done((bf16[256,512]{1,0:T(8,128)(2,1)S(1)}, bf16[256,512]{1,0:T(8,128)(2,1)S(1)}, u32[]{:S(2)}, u32[]{:S(2)}) %collective-permute-start.9) | collective-permute-done | bytes 262176 | tf_op jit(solution)/shard_map/ppermute | solution.py:128
  196.8 6.7 %fusion.14 = bf16[256,2048]{1,0:T(8,128)(2,1)} fusion(bf16[2048,2048]{1,0:T(8,128)(2,1)} %pad_maximum_fusion, bf16[256,2048]{1,0:T(8,128)(2,1)S(1)} %copy-done.1, bf16[256,512]{1,0:T(8,128)(2,1)S(1)} %collective-permute-done.9, bf16[256,512]{1,0:T(8,128)(2,1)S(1)} %collective-permute-done.8, bf16[256,512]{1,0:T(8,128)(2,1)S(1)} %collective-permute-done.7, ...), kind=kOutput, calls=%fused_computation.20 | convolution fusion | flops 2153250816 | bytes 11534336 | tf_op jit(solution)/shard_map/dot_general | solution.py:130
  (60 shorter events, 26.0 us)
Async XLA Ops:
  1.9 35.0 %collective-permute-start = (bf16[136,2048]{1,0:T(8,128)(2,1)}, bf16[136,2048]{1,0:T(8,128)(2,1)S(1)}, u32[]{:S(2)}, u32[]{:S(2)}) collective-permute-start(bf16[136,2048]{1,0:T(8,128)(2,1)} %slice.75), channel_id=1, source_target_pairs={{3,7},{7,11},{11,15},{19,23},{23,27},{27,31},{35,39},{39,43},{43,4... | collective-permute-start | bytes 1671176 | tf_op jit(solution)/shard_map/ppermute | solution.py:56
  2.6 42.5 %collective-permute-start.1 = (bf16[136,2048]{1,0:T(8,128)(2,1)}, bf16[136,2048]{1,0:T(8,128)(2,1)}, u32[]{:S(2)}, u32[]{:S(2)}) collective-permute-start(bf16[136,2048]{1,0:T(8,128)(2,1)} %slice.75), channel_id=1, source_target_pairs={{3,6},{7,10},{11,14},{19,22},{23,26},{27,30},{35,38},{39,42},{43,4... | collective-permute-start | bytes 1671176 | tf_op jit(solution)/shard_map/ppermute | solution.py:56
  4.1 41.0 %collective-permute-start.2 = (bf16[136,2048]{1,0:T(8,128)(2,1)}, bf16[136,2048]{1,0:T(8,128)(2,1)}, u32[]{:S(2)}, u32[]{:S(2)}) collective-permute-start(bf16[136,2048]{1,0:T(8,128)(2,1)} %slice.75), channel_id=1, source_target_pairs={{3,5},{7,9},{11,13},{19,21},{23,25},{27,29},{35,37},{39,41},{43,45... | collective-permute-start | bytes 1671176 | tf_op jit(solution)/shard_map/ppermute | solution.py:56
  5.4 39.8 %collective-permute-start.3 = (bf16[136,2048]{1,0:T(8,128)(2,1)}, bf16[136,2048]{1,0:T(8,128)(2,1)}, u32[]{:S(2)}, u32[]{:S(2)}) collective-permute-start(bf16[136,2048]{1,0:T(8,128)(2,1)} %slice.75), channel_id=1, source_target_pairs={{3,4},{7,8},{11,12},{19,20},{23,24},{27,28},{35,36},{39,40},{43,44... | collective-permute-start | bytes 1671176 | tf_op jit(solution)/shard_map/ppermute | solution.py:56
  6.9 33.8 %collective-permute-start.4 = (bf16[256,2048]{1,0:T(8,128)(2,1)}, bf16[256,2048]{1,0:T(8,128)(2,1)S(1)}, u32[]{:S(2)}, u32[]{:S(2)}) collective-permute-start(bf16[256,2048]{1,0:T(8,128)(2,1)} %param.6), channel_id=1, source_target_pairs={{0,2},{1,3},{2,0},{3,1},{4,6},{5,7},{6,4},{7,5},{8,10},{9,11},{10,... | collective-permute-start | bytes 3145736 | tf_op jit(solution)/shard_map/ppermute | solution.py:43
  13.5 6.7 %copy-start.3 = (f32[7,6144]{1,0:T(8,128)S(1)}, f32[7,6144]{1,0:T(8,128)}, u32[]{:S(2)}) copy-start(f32[7,6144]{1,0:T(8,128)} %param.9) | copy-start | bytes 516100
  13.5 7.1 %copy-start.4 = (bf16[128,128]{1,0:T(8,128)(2,1)S(1)}, bf16[128,128]{1,0:T(8,128)(2,1)}, u32[]{:S(2)}) copy-start(bf16[128,128]{1,0:T(8,128)(2,1)} %param.10) | copy-start | bytes 98308
  13.5 7.7 %copy-start.5 = (s32[1,4]{1,0:T(1,128)S(1)}, s32[1,4]{1,0:T(1,128)}, u32[]{:S(2)}) copy-start(s32[1,4]{1,0:T(1,128)} %param.7) | copy-start | bytes 52
  13.5 117.8 %all-to-all-start = ((bf16[16,3,32,2048]{3,2,1,0:T(8,128)(2,1)}), bf16[16,3,32,2048]{3,2,1,0:T(8,128)(2,1)}, u32[]{:S(2)}, u32[]{:S(2)}) async-start(bf16[16,3,32,2048]{3,2,1,0:T(8,128)(2,1)} %stack.2), calls=%async_computation | async-start | bytes 12582912 | tf_op jit(solution)/shard_map/all_to_all | solution.py:68
  32.5 4.4 %copy-start.1 = (bf16[256,2048]{1,0:T(8,128)(2,1)S(1)}, bf16[256,2048]{1,0:T(8,128)(2,1)}, u32[]{:S(2)}) copy-start(bf16[256,2048]{1,0:T(8,128)(2,1)} %param.6) | copy-start | bytes 3145732
  37.0 10.5 %collective-permute-start.6 = (bf16[256,2048]{1,0:T(8,128)(2,1)S(1)}, bf16[256,2048]{1,0:T(8,128)(2,1)S(1)}, u32[]{:S(2)}, u32[]{:S(2)}) collective-permute-start(bf16[256,2048]{1,0:T(8,128)(2,1)S(1)} %copy-done.1), channel_id=1, source_target_pairs={{0,1},{1,0},{2,3},{3,2},{4,5},{5,4},{6,7},{7,6},{8,9},{9,8},{10,11... | collective-permute-start | bytes 3145736 | tf_op jit(solution)/shard_map/ppermute | solution.py:41
  40.6 6.8 %collective-permute-start.5 = (bf16[256,2048]{1,0:T(8,128)(2,1)S(1)}, bf16[256,2048]{1,0:T(8,128)(2,1)S(1)}, u32[]{:S(2)}, u32[]{:S(2)}) collective-permute-start(bf16[256,2048]{1,0:T(8,128)(2,1)S(1)} %collective-permute-done.4), channel_id=1, source_target_pairs={{0,1},{1,0},{2,3},{3,2},{4,5},{5,4},{6,7},{7,6},{8,9},{9,8},{10,11... | collective-permute-start | bytes 3145736 | tf_op jit(solution)/shard_map/ppermute | solution.py:44
  153.2 2.9 %copy-start = (f32[1152,1536]{1,0:T(8,128)}, f32[1152,1536]{1,0:T(8,128)S(1)}, u32[]{:S(2)}) copy-start(f32[1152,1536]{1,0:T(8,128)S(1)} %multiply_add_fusion) | copy-start | bytes 21233668
  163.2 5.8 %copy-start.2 = (bf16[32,128,128]{2,1,0:T(8,128)(2,1)S(1)}, bf16[32,128,128]{2,1,0:T(8,128)(2,1)}, u32[]{:S(2)}) copy-start(bf16[32,128,128]{2,1,0:T(8,128)(2,1)} %copy.20) | copy-start | bytes 3145732
  181.7 3.2 %collective-permute-start.7 = (bf16[256,512]{1,0:T(8,128)(2,1)S(1)}, bf16[256,512]{1,0:T(8,128)(2,1)S(1)}, u32[]{:S(2)}, u32[]{:S(2)}) collective-permute-start(bf16[256,512]{1,0:T(8,128)(2,1)S(1)} %get-tuple-element.18), channel_id=1, source_target_pairs={{0,1},{1,0},{2,3},{3,2},{4,5},{5,4},{6,7},{7,6},{8,9},{9,8},{10,11... | collective-permute-start | bytes 786440 | tf_op jit(solution)/shard_map/ppermute | solution.py:128
  183.1 7.9 %collective-permute-start.8 = (bf16[256,512]{1,0:T(8,128)(2,1)S(1)}, bf16[256,512]{1,0:T(8,128)(2,1)S(1)}, u32[]{:S(2)}, u32[]{:S(2)}) collective-permute-start(bf16[256,512]{1,0:T(8,128)(2,1)S(1)} %get-tuple-element.17), channel_id=1, source_target_pairs={{0,2},{1,3},{2,0},{3,1},{4,6},{5,7},{6,4},{7,5},{8,10},{9,11},{10,... | collective-permute-start | bytes 786440 | tf_op jit(solution)/shard_map/ppermute | solution.py:128
  183.1 13.7 %collective-permute-start.9 = (bf16[256,512]{1,0:T(8,128)(2,1)S(1)}, bf16[256,512]{1,0:T(8,128)(2,1)S(1)}, u32[]{:S(2)}, u32[]{:S(2)}) collective-permute-start(bf16[256,512]{1,0:T(8,128)(2,1)S(1)} %get-tuple-element.16), channel_id=1, source_target_pairs={{0,3},{1,2},{2,1},{3,0},{4,7},{5,6},{6,5},{7,4},{8,11},{9,10},{10,... | collective-permute-start | bytes 786440 | tf_op jit(solution)/shard_map/ppermute | solution.py:128
